TPU v7x, 256 devices: a whole 4x4x8 slice. The times are simulated.
256 devices in a mesh: ta: 8 (over x_lo, y), gx: 4 (over x_hi, core), yz: 8 (over z).
Axes of the slice: x: 4 (x_hi: 2, x_lo: 2; x = x_hi * 2 + x_lo), y: 4, z: 8, core: 2. Of those that a mesh axis runs over, the one named last changes fastest.
Arguments:
- vectors: bfloat16 [2, 3, 32, 64, 256, 128], P(None, None, 'gx', 'yz', 'ta'), parts along dimension 4, may hold values from -6 to 6
- gauge_x: float32 [2, 3, 3, 32, 64, 256], P(None, None, None, 'gx', 'yz', 'ta'), parts along dimension 5, may hold values from -6 to 6
- gauge_y: float32 [2, 3, 3, 32, 64, 256], P(None, None, None, 'gx', 'yz', 'ta'), parts along dimension 5, may hold values from -6 to 6
Outputs:
- elementals: float32 [16, 2, 128, 128], P('ta'), parts along dimension 0
There are 8 independent parts, one for each index of `ta`. A program takes and returns all parts, laid end to end along the dimension named above; each array names one. Nothing has to cross between parts.
All inputs are finite; a program needn't handle non-finite values.
Results may differ from a plain program's by a relative error of at most 0.0029.
Values may be sent and summed in bfloat16 or wider, within the bound.
No kernel may reach another device: no remote copies, remote signals or barrier semaphores. Data moves between devices by JAX's collectives and lax.ppermute only.
A program may use at most 64 MiB of HBM per device.

v0:
```python
import math
import jax
import jax.numpy as jnp
from jax import lax
from jax.sharding import PartitionSpec as P


def shifted(value, axis, steps):
    count = lax.axis_size(axis)
    pairs = [(source, (source + steps) % count) for source in range(count)]
    return lax.ppermute(value, axis, pairs)


def colour_apply(gauge, source_vectors):
    real_parts = []
    imag_parts = []
    for colour in range(3):
        real_running = jnp.zeros(source_vectors.shape[2:], jnp.float32)
        imaginary_running = jnp.zeros(source_vectors.shape[2:], jnp.float32)
        for inner_product in range(3):
            left_real = gauge[0, colour, inner_product][..., None]
            left_imaginary = gauge[1, colour, inner_product][..., None]
            right_real = source_vectors[0, inner_product].astype(jnp.float32)
            right_imaginary = source_vectors[1, inner_product].astype(jnp.float32)
            real_running = real_running + left_real * right_real - left_imaginary * right_imaginary
            imaginary_running = (
                imaginary_running + left_real * right_imaginary + left_imaginary * right_real
            )
        real_parts.append(real_running)
        imag_parts.append(imaginary_running)
    return jnp.stack([jnp.stack(real_parts), jnp.stack(imag_parts)]).astype(jnp.bfloat16)


def right_block(image):
    nvecs = image.shape[-1]
    real_rows = image[0].reshape(-1, nvecs)
    imag_rows = image[1].reshape(-1, nvecs)
    first = jnp.concatenate([real_rows, imag_rows], 0)
    second = jnp.concatenate([imag_rows, -real_rows], 0)
    return (first, second)


def contract(left_cols, right_cols):
    return lax.dot_general(
        left_cols, right_cols, (((0,), (0,)), ((), ())), preferred_element_type=jnp.float32
    )


def local(vectors, gauge_x, gauge_y):
    nvecs = vectors.shape[-1]
    from_next_x = shifted(vectors[:, :, :1], "gx", -1)
    shifted_x = jnp.concatenate([vectors[:, :, 1:], from_next_x], 2)
    from_next_y = shifted(vectors[:, :, :, :1], "yz", -1)
    shifted_y = jnp.concatenate([vectors[:, :, :, 1:], from_next_y], 3)
    image_x = colour_apply(gauge_x, shifted_x)
    image_y = colour_apply(gauge_y, shifted_y)
    left_rows = vectors.reshape(-1, nvecs)
    blocks = right_block(image_x) + right_block(image_y)
    summed = lax.psum(
        jnp.concatenate([contract(left_rows, member) for member in blocks], 1), ("gx", "yz")
    )
    sites_total = (
        vectors.shape[2]
        * lax.axis_size("gx")
        * vectors.shape[3]
        * lax.axis_size("yz")
        * vectors.shape[4]
    )
    scaling = 1.0 / math.sqrt(3.0 * sites_total)
    return (summed * scaling).reshape(nvecs, 2, 2, nvecs).transpose(1, 2, 0, 3)


def solution(mesh):
    placed = (
        P(None, None, "gx", "yz", "ta", None),
        P(None, None, None, "gx", "yz", "ta"),
        P(None, None, None, "gx", "yz", "ta"),
    )
    return jax.shard_map(
        local, mesh=mesh, in_specs=placed, out_specs=P("ta", None, None, None), check_vma=False
    )
```

profile of v0, /device:TPU:8, one launch (start us, length us, event | category | flops | bytes accessed | tf_op | source)
XLA Modules:
  0.0 315.3 jit_solution(16234775033811610859)
XLA Ops:
  6.5 0.0 all-reduce.2.cloned.1.call-start
  6.5 1.0 slice.186
  7.6 0.0 copy-start
  7.6 2.5 collective-permute-start
  10.1 1.0 slice.212
  11.1 5.9 %collective-permute-start.1 = (bf16[2,3,8,1,32,128]{5,4,3,2,1,0:T(8,128)(2,1)S(1)}, bf16[2,3,8,1,32,128]{5,4,3,2,1,0:T(8,128)(2,1)S(1)}, u32[]{:S(2)}, u32[]{:S(2)}) collective-permute-start(bf16[2,3,8,1,32,128]{5,4,3,2,1,0:T(8,128)(2,1)S(1)} %slice.212), channel_id=1, source_target_pairs={{0,7},{1,0},{2,1},{3,2},{4,3},{5,4},{6,5},{7,6},{8,15},{9,8},{10,9... | collective-permute-start | bytes 1179656 | tf_op jit(solution)/shard_map/ppermute | solution.py:11
  17.1 0.0 copy-done
  17.1 0.0 copy-start.1
  17.1 0.0 copy-start.2
  17.1 0.0 slice-start
  17.1 0.7 slice.211
  17.8 0.4 copy-done.1
  18.2 0.1 copy-done.2
  18.4 0.0 collective-permute-done
  18.4 0.8 slice-done
  19.2 2.1 fusion.51
  21.3 1.9 fusion.33
  23.3 3.9 %fusion.57 = (bf16[1,8,8,32,128]{4,3,2,1,0:T(8,128)(2,1)S(1)}, bf16[1,8,8,32,128]{4,3,2,1,0:T(8,128)(2,1)S(1)}, bf16[1,8,8,32,128]{4,3,2,1,0:T(8,128)(2,1)S(1)}, bf16[1,8,8,32,128]{4,3,2,1,0:T(8,128)(2,1)S(1)}) fusion(bf16[1,8,8,32,128]{4,3,2,1,0:T(8,128)(2,1)S(1)} %get-tuple-element.11, bf16[1,8,8,32,128]{4,3,2,1,0:T(8,128)(2,1)S(1)} %get-tuple-element.10, ...), kind=kLoop, calls=%fused_computation.145 | loop fusion | flops 14155776 | bytes 5341184 | tf_op jit(solution)/shard_map/convert.26
  27.2 0.3 pad_maximum_fusion
  27.5 0.3 bitcast_negate_fusion.1
  27.8 1.0 fusion.25
  28.9 1.0 fusion.22
  29.9 0.0 collective-permute-done.1
  29.9 2.0 fusion.87
  31.9 1.9 fusion.69
  33.9 3.9 %fusion.93 = (bf16[1,8,8,32,128]{4,3,2,1,0:T(8,128)(2,1)S(1)}, bf16[1,8,8,32,128]{4,3,2,1,0:T(8,128)(2,1)S(1)}, bf16[1,8,8,32,128]{4,3,2,1,0:T(8,128)(2,1)S(1)}, bf16[1,8,8,32,128]{4,3,2,1,0:T(8,128)(2,1)S(1)}) fusion(bf16[1,8,8,32,128]{4,3,2,1,0:T(8,128)(2,1)S(1)} %get-tuple-element.18, bf16[1,8,8,32,128]{4,3,2,1,0:T(8,128)(2,1)S(1)} %get-tuple-element.17, ...), kind=kLoop, calls=%fused_computation.181 | loop fusion | flops 14155776 | bytes 5341184 | tf_op jit(solution)/shard_map/convert.16
  37.8 0.3 pad_maximum_fusion.2
  38.2 0.3 bitcast_negate_fusion
  38.5 1.0 fusion.19
  39.5 1.1 fusion.16
  40.6 0.7 pad_maximum_fusion.6
  41.3 0.0 all-reduce.2.cloned.1.call-update
  41.3 265.3 %all-reduce.2.cloned.1.call-done = f32[128,512]{0,1:T(8,128)} async-done(((f32[128,512]{0,1:T(8,128)}), f32[128,512]{0,1:T(8,128)}) %all-reduce.2.cloned.1.call-update) | async-done | bytes 262160 | tf_op jit(solution)/shard_map/psum | solution.py:59
  306.6 1.0 broadcast_multiply_fusion
  307.6 0.8 copy.4
  (2 shorter events, 0.1 us)
Async XLA Ops:
  6.5 300.1 %all-reduce.2.cloned.1.call-start = ((), (), s32[]{:S(2)}) async-start(), calls=%async_computation | async-start | bytes 524288 | tf_op jit(solution)/shard_map/psum | solution.py:59
  7.6 9.5 %copy-start = (bf16[2,3,8,8,32,128]{5,4,3,2,1,0:T(8,128)(2,1)S(1)}, bf16[2,3,8,8,32,128]{5,4,3,2,1,0:T(8,128)(2,1)}, u32[]{:S(2)}) copy-start(bf16[2,3,8,8,32,128]{5,4,3,2,1,0:T(8,128)(2,1)} %param.3) | copy-start | bytes 9437188
  7.6 10.8 %collective-permute-start = (bf16[2,3,1,8,32,128]{5,4,3,2,1,0:T(8,128)(2,1)S(1)}, bf16[2,3,1,8,32,128]{5,4,3,2,1,0:T(8,128)(2,1)S(1)}, u32[]{:S(2)}, u32[]{:S(2)}) collective-permute-start(bf16[2,3,1,8,32,128]{5,4,3,2,1,0:T(8,128)(2,1)S(1)} %slice.186), channel_id=1, source_target_pairs={{0,24},{8,0},{16,8},{24,16},{1,25},{9,1},{17,9},{25,17},{2,26},{10... | collective-permute-start | bytes 1179656 | tf_op jit(solution)/shard_map/ppermute | solution.py:11
  11.1 18.8 %collective-permute-start.1 = (bf16[2,3,8,1,32,128]{5,4,3,2,1,0:T(8,128)(2,1)S(1)}, bf16[2,3,8,1,32,128]{5,4,3,2,1,0:T(8,128)(2,1)S(1)}, u32[]{:S(2)}, u32[]{:S(2)}) collective-permute-start(bf16[2,3,8,1,32,128]{5,4,3,2,1,0:T(8,128)(2,1)S(1)} %slice.212), channel_id=1, source_target_pairs={{0,7},{1,0},{2,1},{3,2},{4,3},{5,4},{6,5},{7,6},{8,15},{9,8},{10,9... | collective-permute-start | bytes 1179656 | tf_op jit(solution)/shard_map/ppermute | solution.py:11
  17.1 1.1 copy-start.1
  17.1 1.2 copy-start.2
  17.1 2.1 slice-start
Sparse Core Ops, SparseCore 0:
  41.5 265.1 all-reduce.1
where the time goes:
time: 315 us
  waiting for transfers between devices  265 us (84%)
  other arithmetic  18.8 us (6%)
  between operations  13.6 us (4%)
  starting transfers between devices  8.47 us (3%)
  local copies, waits for them, and re-layouts  5 us (2%)
  matrix products  4.18 us (1%)
    psum x1, waiting for transfers between devices, local(): lax.psum(jnp.concatenate([contract(left_rows, member) for member in block...  265 us
    another operation x6, other arithmetic  15.8 us
    ppermute x2, starting transfers between devices, shifted(): return lax.ppermute(value, axis, pairs)  8.47 us
  transfers between devices with their start and end apart: 3, of which 1 were waited for; matrix products, arithmetic and copies ran while one was open for 4% of the time, Pallas kernels for 0%

commit v1 on v0

--- a/solution.py
+++ b/solution.py
@@ -56,8 +56,11 @@
     image_y = colour_apply(gauge_y, shifted_y)
     left_rows = vectors.reshape(-1, nvecs)
     blocks = right_block(image_x) + right_block(image_y)
-    summed = lax.psum(
-        jnp.concatenate([contract(left_rows, member) for member in blocks], 1), ("gx", "yz")
+    summed = jnp.sum(
+        lax.all_gather(
+            jnp.concatenate([contract(left_rows, member) for member in blocks], 1), ("gx", "yz")
+        ),
+        axis=0,
     )
     sites_total = (
         vectors.shape[2]

time: 315 us -> 167 us (0.53)
  waiting for transfers between devices: 265 us -> 111 us
  local copies, waits for them, and re-layouts: 5 us -> 9.37 us
    psum x1 -> x0, waiting for transfers between devices: 265 us -> none  [local(): lax.psum(jnp.concatenate([contract(left_rows, member) for member in block...]
    all_gather x0 -> x1, waiting for transfers between devices: none -> 107 us  [local(): lax.all_gather(jnp.concatenate([contract(left_rows, member) for member in...]
    unnamed x6 -> x7, local copies, waits for them, and re-layouts: 0.49 us -> 5.7 us
    ppermute x2, waiting for transfers between devices: 0.01 us -> 4 us  [shifted(): return lax.ppermute(value, axis, pairs)]
  transfers between devices with their start and end apart: 3 -> 3, of which waited for: 1 -> 2; matrix products, arithmetic and copies ran while one was open for 4% -> 8% of each run, Pallas kernels for 0% -> 0%
where the time goes in v1:
time: 167 us; the launch traced here: 165 us
  waiting for transfers between devices  111 us (66%)
  other arithmetic  19.4 us (12%)
  between operations  13.6 us (8%)
  local copies, waits for them, and re-layouts  9.37 us (6%)
  starting transfers between devices  8.2 us (5%)
  matrix products  4.18 us (3%)
    all_gather x1, waiting for transfers between devices, local(): lax.all_gather(jnp.concatenate([contract(left_rows, member) for member in...  107 us
    another operation x6, other arithmetic  15.8 us
    ppermute x2, starting transfers between devices, shifted(): return lax.ppermute(value, axis, pairs)  8.19 us
    unnamed x7, local copies, waits for them, and re-layouts  5.7 us
    dot_general x4, matrix products, contract(): lax.dot_general(left_cols, right_cols, (((0,), (0,)), ((), ())), preferre...  4.18 us
    ppermute x2, waiting for transfers between devices, shifted(): return lax.ppermute(value, axis, pairs)  4 us
  transfers between devices with their start and end apart: 3, of which 2 were waited for; matrix products, arithmetic and copies ran while one was open for 8% of the time, Pallas kernels for 0%

profile of v1, /device:TPU:8, one launch (start us, length us, event | category | flops | bytes accessed | tf_op | source)
XLA Modules:
  0.0 165.4 jit_solution(16270096715547627542)
XLA Ops:
  6.5 0.0 all-gather.3.cloned.1.call-start
  6.5 1.0 slice.212
  7.6 0.0 copy-start
  7.6 5.9 %collective-permute-start.1 = (bf16[2,3,8,1,32,128]{5,4,3,2,1,0:T(8,128)(2,1)S(1)}, bf16[2,3,8,1,32,128]{5,4,3,2,1,0:T(8,128)(2,1)S(1)}, u32[]{:S(2)}, u32[]{:S(2)}) collective-permute-start(bf16[2,3,8,1,32,128]{5,4,3,2,1,0:T(8,128)(2,1)S(1)} %slice.212), channel_id=1, source_target_pairs={{0,7},{1,0},{2,1},{3,2},{4,3},{5,4},{6,5},{7,6},{8,15},{9,8},{10,9... | collective-permute-start | bytes 1179656 | tf_op jit(solution)/shard_map/ppermute | solution.py:11
  13.5 1.0 slice.186
  14.5 2.3 %collective-permute-start = (bf16[2,3,1,8,32,128]{5,4,3,2,1,0:T(8,128)(2,1)S(1)}, bf16[2,3,1,8,32,128]{5,4,3,2,1,0:T(8,128)(2,1)S(1)}, u32[]{:S(2)}, u32[]{:S(2)}) collective-permute-start(bf16[2,3,1,8,32,128]{5,4,3,2,1,0:T(8,128)(2,1)S(1)} %slice.186), channel_id=1, source_target_pairs={{0,24},{8,0},{16,8},{24,16},{1,25},{9,1},{17,9},{25,17},{2,26},{10... | collective-permute-start | bytes 1179656 | tf_op jit(solution)/shard_map/ppermute | solution.py:11
  16.8 0.0 copy-done
  16.8 0.0 copy-start.1
  16.8 0.0 copy-start.2
  16.8 0.0 slice-start
  16.8 0.7 slice.211
  17.5 0.4 copy-done.1
  17.9 0.1 copy-done.2
  18.1 4.0 %collective-permute-done = bf16[2,3,1,8,32,128]{5,4,3,2,1,0:T(8,128)(2,1)S(1)} collective-permute-done((bf16[2,3,1,8,32,128]{5,4,3,2,1,0:T(8,128)(2,1)S(1)}, bf16[2,3,1,8,32,128]{5,4,3,2,1,0:T(8,128)(2,1)S(1)}, u32[]{:S(2)}, u32[]{:S(2)}) %collective-permute-start) | collective-permute-done | bytes 393248 | tf_op jit(solution)/shard_map/ppermute | solution.py:11
  22.1 0.0 slice-done
  22.1 2.1 %fusion.51 = (bf16[1,8,8,32,128]{4,3,2,1,0:T(8,128)(2,1)S(1)}, bf16[1,8,8,32,128]{4,3,2,1,0:T(8,128)(2,1)S(1)}, bf16[1,8,8,32,128]{4,3,2,1,0:T(8,128)(2,1)S(1)},...) fusion(f32[8,8,32]{2,1,0:T(8,128)S(1)} %get-tuple-element.41, ...), kind=kLoop, calls=%fused_computation.140 | loop fusion | flops 6291456 | bytes 6864896 | tf_op jit(solution)/shard_map/convert.25
  24.2 1.9 %fusion.33 = bf16[1,8,8,32,128]{4,3,2,1,0:T(8,128)(2,1)S(1)} fusion(bf16[1,8,8,32,128]{4,3,2,1,0:T(8,128)(2,1)S(1)} %get-tuple-element.11, bf16[1,8,8,32,128]{4,3,2,1,0:T(8,128)(2,1)S(1)} %get-tuple-element.10, bf16[1,8,8,32,128]{4,3,2,1,0:T(8,128)(2,1)S(1)} %get-tuple-element.9, bf16[1,8,8,32,128]{4,3,2,1,0:T(8,128)(2,1)S(1)} %get-tuple-element.8, ...), kind=kLoop, calls=%fused_computation.122 | loop fusion | flops 4718592 | bytes 3719168 | tf_op jit(solution)/shard_map/convert.29
  26.1 3.9 %fusion.57 = (bf16[1,8,8,32,128]{4,3,2,1,0:T(8,128)(2,1)S(1)}, bf16[1,8,8,32,128]{4,3,2,1,0:T(8,128)(2,1)S(1)}, bf16[1,8,8,32,128]{4,3,2,1,0:T(8,128)(2,1)S(1)}, bf16[1,8,8,32,128]{4,3,2,1,0:T(8,128)(2,1)S(1)}) fusion(bf16[1,8,8,32,128]{4,3,2,1,0:T(8,128)(2,1)S(1)} %get-tuple-element.11, bf16[1,8,8,32,128]{4,3,2,1,0:T(8,128)(2,1)S(1)} %get-tuple-element.10, ...), kind=kLoop, calls=%fused_computation.146 | loop fusion | flops 14155776 | bytes 5341184 | tf_op jit(solution)/shard_map/convert.26
  30.0 0.3 pad_maximum_fusion
  30.4 0.3 bitcast_negate_fusion.1
  30.7 1.0 fusion.25
  31.8 1.0 fusion.22
  32.8 0.0 collective-permute-done.1
  32.8 2.0 %fusion.87 = (bf16[1,8,8,32,128]{4,3,2,1,0:T(8,128)(2,1)S(1)}, bf16[1,8,8,32,128]{4,3,2,1,0:T(8,128)(2,1)S(1)}, bf16[1,8,8,32,128]{4,3,2,1,0:T(8,128)(2,1)S(1)},...) fusion(f32[8,8,32]{2,1,0:T(8,128)S(1)} %get-tuple-element.59, ...), kind=kLoop, calls=%fused_computation.176 | loop fusion | flops 6291456 | bytes 6864896 | tf_op jit(solution)/shard_map/convert.15
  34.8 1.9 %fusion.69 = bf16[1,8,8,32,128]{4,3,2,1,0:T(8,128)(2,1)S(1)} fusion(bf16[1,8,8,32,128]{4,3,2,1,0:T(8,128)(2,1)S(1)} %get-tuple-element.18, bf16[1,8,8,32,128]{4,3,2,1,0:T(8,128)(2,1)S(1)} %get-tuple-element.17, bf16[1,8,8,32,128]{4,3,2,1,0:T(8,128)(2,1)S(1)} %get-tuple-element.16, bf16[1,8,8,32,128]{4,3,2,1,0:T(8,128)(2,1)S(1)} %get-tuple-element.15, ...), kind=kLoop, calls=%fused_computation.158 | loop fusion | flops 4718592 | bytes 3719168 | tf_op jit(solution)/shard_map/convert.19
  36.8 3.9 %fusion.93 = (bf16[1,8,8,32,128]{4,3,2,1,0:T(8,128)(2,1)S(1)}, bf16[1,8,8,32,128]{4,3,2,1,0:T(8,128)(2,1)S(1)}, bf16[1,8,8,32,128]{4,3,2,1,0:T(8,128)(2,1)S(1)}, bf16[1,8,8,32,128]{4,3,2,1,0:T(8,128)(2,1)S(1)}) fusion(bf16[1,8,8,32,128]{4,3,2,1,0:T(8,128)(2,1)S(1)} %get-tuple-element.18, bf16[1,8,8,32,128]{4,3,2,1,0:T(8,128)(2,1)S(1)} %get-tuple-element.17, ...), kind=kLoop, calls=%fused_computation.182 | loop fusion | flops 14155776 | bytes 5341184 | tf_op jit(solution)/shard_map/convert.16
  40.7 0.3 pad_maximum_fusion.2
  41.0 0.3 bitcast_negate_fusion
  41.4 1.0 fusion.19
  42.4 1.1 fusion.16
  43.5 0.7 pad_maximum_fusion.6
  44.2 0.0 all-gather.3.cloned.1.call-update
  44.2 106.7 %all-gather.3.cloned.1.call-done = f32[4096,512]{0,1:T(8,128)} async-done(((f32[128,512]{0,1:T(8,128)}), f32[4096,512]{0,1:T(8,128)}) %all-gather.3.cloned.1.call-update) | async-done | bytes 8388624 | tf_op jit(solution)/shard_map/all_gather | solution.py:60
  150.9 5.2 %copy.5 = f32[64,8,32,128]{3,2,1,0:T(8,128)S(1)} copy(f32[64,8,32,128]{3,1,2,0:T(8,128)} %bitcast.151) | data formatting | bytes 16777216
  156.1 1.6 bitcast_reduce_fusion
  157.7 0.8 copy.4
  (3 shorter events, 0.1 us)
Async XLA Ops:
  6.5 144.3 %all-gather.3.cloned.1.call-start = ((), (), s32[]{:S(2)}) async-start(), calls=%async_computation | async-start | bytes 8650752 | tf_op jit(solution)/shard_map/all_gather | solution.py:60
  7.6 9.2 %copy-start = (bf16[2,3,8,8,32,128]{5,4,3,2,1,0:T(8,128)(2,1)S(1)}, bf16[2,3,8,8,32,128]{5,4,3,2,1,0:T(8,128)(2,1)}, u32[]{:S(2)}) copy-start(bf16[2,3,8,8,32,128]{5,4,3,2,1,0:T(8,128)(2,1)} %param.3) | copy-start | bytes 9437188
  7.6 25.2 %collective-permute-start.1 = (bf16[2,3,8,1,32,128]{5,4,3,2,1,0:T(8,128)(2,1)S(1)}, bf16[2,3,8,1,32,128]{5,4,3,2,1,0:T(8,128)(2,1)S(1)}, u32[]{:S(2)}, u32[]{:S(2)}) collective-permute-start(bf16[2,3,8,1,32,128]{5,4,3,2,1,0:T(8,128)(2,1)S(1)} %slice.212), channel_id=1, source_target_pairs={{0,7},{1,0},{2,1},{3,2},{4,3},{5,4},{6,5},{7,6},{8,15},{9,8},{10,9... | collective-permute-start | bytes 1179656 | tf_op jit(solution)/shard_map/ppermute | solution.py:11
  14.5 7.6 %collective-permute-start = (bf16[2,3,1,8,32,128]{5,4,3,2,1,0:T(8,128)(2,1)S(1)}, bf16[2,3,1,8,32,128]{5,4,3,2,1,0:T(8,128)(2,1)S(1)}, u32[]{:S(2)}, u32[]{:S(2)}) collective-permute-start(bf16[2,3,1,8,32,128]{5,4,3,2,1,0:T(8,128)(2,1)S(1)} %slice.186), channel_id=1, source_target_pairs={{0,24},{8,0},{16,8},{24,16},{1,25},{9,1},{17,9},{25,17},{2,26},{10... | collective-permute-start | bytes 1179656 | tf_op jit(solution)/shard_map/ppermute | solution.py:11
  16.8 1.1 copy-start.1
  16.8 1.2 copy-start.2
  16.8 5.3 %slice-start = ((bf16[2,3,8,8,32,128]{5,4,3,2,1,0:T(8,128)(2,1)}), bf16[2,3,7,8,32,128]{5,4,3,2,1,0:T(8,128)(2,1)S(1)}, s32[]{:S(2)}) async-start(bf16[2,3,8,8,32,128]{5,4,3,2,1,0:T(8,128)(2,1)} %param.3), calls=%async_computation.1 | async-start | bytes 5505024 | tf_op jit(solution)/shard_map/slice | solution.py:52
Sparse Core Ops, SparseCore 0:
  44.3 106.4 all-gather.2
